TPU v7x, 256 devices: a whole 4x4x8 slice. The times are simulated.
256 devices in a mesh: ctx: 64 (over x, y_hi, z), pipe: 4 (over y_lo, core).
Axes of the slice: x: 4, y: 4 (y_hi: 2, y_lo: 2; y = y_hi * 2 + y_lo), z: 8, core: 2. Of those that a mesh axis runs over, the one named last changes fastest.
Arguments:
- inputs: bfloat16 [4, 8192, 4096], P('pipe', 'ctx'), may hold values from -16 to 16
- q_raw: bfloat16 [4, 8192, 2048], P('pipe', 'ctx'), may hold values from -6 to 6
- grad_out: bfloat16 [4, 8192, 2048], P('pipe', 'ctx'), may hold values from -6 to 6
- segments: int32 [4, 8192], P('pipe'), may hold values from 0 to 4, never falling along the last dimension, each value on 1 to 3072 neighbouring positions
- w_key: bfloat16 [4, 4096, 512], P('pipe', 'ctx'), may hold values from -0.09375 to 0.09375
- w_value: bfloat16 [4, 4096, 512], P('pipe', 'ctx'), may hold values from -0.09375 to 0.09375
- q_gain: float32 [4, 128], P('pipe'), may hold values from 0.1 to 1.9
- k_gain: float32 [4, 128], P('pipe'), may hold values from 0.1 to 1.9
Outputs:
- query_grad: bfloat16 [4, 8192, 2048], P('pipe', 'ctx')
- key_weight_grad: float32 [4, 4096, 512], P('pipe', 'ctx')
- value_weight_grad: float32 [4, 4096, 512], P('pipe', 'ctx')
- section_grad: bfloat16 [4, 8192, 4096], P('pipe', 'ctx')
Inputs may be any that keep to these rules, and one draw needn't show every extreme that they name: `segments`: along each section's sequence the document numbers never fall; every document has 1 to 3072 tokens and one has exactly 3072.
All inputs are finite; a program needn't handle non-finite values.
Results may differ from a plain program's by a relative error of at most 0.019.
Values may be sent and summed in bfloat16 or wider, within the bound.
No kernel may reach another device: no remote copies, remote signals or barrier semaphores. Data moves between devices by JAX's collectives and lax.ppermute only.
A program may use at most 128 MiB of HBM per device.

v0:
```python
import jax
import jax.numpy as jnp
from jax import lax
from jax.sharding import PartitionSpec as P

HEAD = 128
WINDOW = 768
epsilon = 1e-06
theta_base = 1000000.0


def passed_along(block, axis, distance):
    devices = range(lax.axis_size(axis))
    route = [(i - distance, i) for i in devices if i - distance in devices]
    return lax.ppermute(block, axis, route)


def shifted(shard, axis, by):
    devices = lax.axis_size(axis)
    return lax.ppermute(shard, axis, [(i, (i + by) % devices) for i in range(devices)])


def rope_tables(positions):
    half_width = HEAD // 2
    frequency = jnp.exp(
        jnp.arange(half_width, dtype=jnp.float32) * (-2.0 * jnp.log(jnp.float32(theta_base)) / HEAD)
    )
    angles = positions.astype(jnp.float32)[:, None] * frequency[None, :]
    return (jnp.cos(angles), jnp.sin(angles))


def rotate(values, cosine, sine_table):
    half_width = values.shape[-1] // 2
    front_half = values[..., :half_width]
    back_half = values[..., half_width:]
    cos_b = cosine[:, None, :]
    sin_b = sine_table[:, None, :]
    return jnp.concatenate(
        [front_half * cos_b - back_half * sin_b, back_half * cos_b + front_half * sin_b], -1
    )


def unrotate(upstream, cosine, sine_table):
    half_width = upstream.shape[-1] // 2
    front_half = upstream[..., :half_width]
    back_half = upstream[..., half_width:]
    cos_b = cosine[:, None, :]
    sin_b = sine_table[:, None, :]
    return jnp.concatenate(
        [front_half * cos_b + back_half * sin_b, back_half * cos_b - front_half * sin_b], -1
    )


def normalize(values, gain_row):
    inverse = lax.rsqrt(jnp.mean(values * values, -1, keepdims=True) + epsilon)
    return (values * inverse * gain_row, inverse)


def normalize_back(values, inverse, gain_row, upstream):
    scaled = upstream * gain_row
    cubed = inverse * inverse * inverse
    return inverse * scaled - values * cubed * jnp.mean(values * scaled, -1, keepdims=True)


def guarded(tile_work, operands):
    return tile_work(*operands)


def local(inputs, q_raw, grad_out, segments, w_key, w_value, q_gain, k_gain):
    tokens_here = inputs[0]
    tok_rows = tokens_here.shape[0]
    kv_width = w_key.shape[2]
    kv_heads = kv_width // HEAD
    q_heads = q_raw.shape[2] // HEAD
    group = q_heads // kv_heads
    score_scale = HEAD ** (-0.5)
    reach_blocks = WINDOW // tok_rows
    ctx_index = lax.axis_index("ctx")
    key_full, value_full = (
        lax.all_gather(w_key[0], "ctx", axis=0, tiled=True),
        lax.all_gather(w_value[0], "ctx", axis=0, tiled=True),
    )
    key_raw = jnp.dot(tokens_here, key_full, preferred_element_type=jnp.float32).astype(
        jnp.bfloat16
    )
    value_own = (
        jnp.dot(tokens_here, value_full, preferred_element_type=jnp.float32)
        .astype(jnp.bfloat16)
        .reshape(tok_rows, kv_heads, HEAD)
    )
    local_pos = jnp.arange(tok_rows, dtype=jnp.int32)
    positions = ctx_index * tok_rows + local_pos
    cosine, sine_table = rope_tables(positions)
    query_in = q_raw[0].astype(jnp.float32).reshape(tok_rows, q_heads, HEAD)
    query_norm, query_inv = normalize(query_in, q_gain[0])
    query_rot = rotate(query_norm, cosine, sine_table).astype(jnp.bfloat16)
    key_in = key_raw.astype(jnp.float32).reshape(tok_rows, kv_heads, HEAD)
    key_norm, key_inv = normalize(key_in, k_gain[0])
    key_rot = rotate(key_norm, cosine, sine_table).astype(jnp.bfloat16)
    own_pair = jnp.stack([key_rot, value_own])
    key_blocks = [own_pair]
    for distance in range(1, reach_blocks + 1):
        key_blocks.append(passed_along(own_pair, "ctx", distance))
    seg_all = segments[0]
    seg_query = lax.dynamic_slice_in_dim(seg_all, ctx_index * tok_rows, tok_rows)
    allowed_list = []
    for distance in range(reach_blocks + 1):
        key_pos = (ctx_index - distance) * tok_rows + local_pos
        seg_key = lax.dynamic_slice_in_dim(
            seg_all, jnp.maximum(ctx_index - distance, 0) * tok_rows, tok_rows
        )
        offset = positions[:, None] - key_pos[None, :]
        allowed = (
            (offset >= 0)
            & (offset < WINDOW)
            & (key_pos >= 0)[None, :]
            & (seg_query[:, None] == seg_key[None, :])
        )
        allowed_list.append(allowed)
    q_group = query_rot.reshape(tok_rows, kv_heads, group, HEAD)
    out_grad = grad_out[0].reshape(tok_rows, kv_heads, group, HEAD)

    def exp_block(key_pair, allowed):
        scores = (
            jnp.einsum("qgrd,kgd->grqk", q_group, key_pair[0], preferred_element_type=jnp.float32)
            * score_scale
        )
        return jnp.where(allowed, jnp.exp(scores), 0.0)

    def total_block(key_pair, allowed):
        return jnp.sum(exp_block(key_pair, allowed), -1)

    zero_total = jnp.zeros((kv_heads, group, tok_rows), jnp.float32)
    row_total = zero_total
    for distance in range(reach_blocks + 1):
        row_total = row_total + guarded(total_block, (key_blocks[distance], allowed_list[distance]))

    def prob_block(key_pair, allowed):
        prob_tile = (exp_block(key_pair, allowed) / row_total[..., None]).astype(jnp.bfloat16)
        out_tile = jnp.einsum(
            "grqk,kgd->qgrd", prob_tile, key_pair[1], preferred_element_type=jnp.float32
        )
        return (prob_tile, out_tile)

    zero_query = jnp.zeros((tok_rows, kv_heads, group, HEAD), jnp.float32)
    prob_list = []
    attn_out = zero_query
    for distance in range(reach_blocks + 1):
        prob_tile, out_tile = guarded(prob_block, (key_blocks[distance], allowed_list[distance]))
        prob_list.append(prob_tile)
        attn_out = attn_out + out_tile
    row_delta = jnp.sum(out_grad.astype(jnp.float32) * attn_out, -1).transpose(1, 2, 0)[..., None]

    def grad_block(key_pair, prob_tile):
        prob_grad = jnp.einsum(
            "qgrd,kgd->grqk", out_grad, key_pair[1], preferred_element_type=jnp.float32
        )
        score_grad = (prob_tile.astype(jnp.float32) * (prob_grad - row_delta)).astype(jnp.bfloat16)
        value_grad = jnp.einsum(
            "grqk,qgrd->kgd", prob_tile, out_grad, preferred_element_type=jnp.float32
        )
        key_grad = (
            jnp.einsum("grqk,qgrd->kgd", score_grad, q_group, preferred_element_type=jnp.float32)
            * score_scale
        )
        query_part = (
            jnp.einsum(
                "grqk,kgd->qgrd", score_grad, key_pair[0], preferred_element_type=jnp.float32
            )
            * score_scale
        )
        return (query_part, jnp.stack([key_grad, value_grad]))

    zero_pair = jnp.zeros((2, tok_rows, kv_heads, HEAD), jnp.float32)
    query_rot_grad = zero_query
    kv_total = zero_pair
    for distance in range(reach_blocks + 1):
        query_part, kv_part = guarded(grad_block, (key_blocks[distance], prob_list[distance]))
        query_rot_grad = query_rot_grad + query_part
        if distance == 0:
            kv_total = kv_part
        else:
            returned = passed_along(kv_part.astype(jnp.bfloat16), "ctx", -distance)
            kv_total = kv_total + returned.astype(jnp.float32)
    query_grad = normalize_back(
        query_in,
        query_inv,
        q_gain[0],
        unrotate(query_rot_grad.reshape(tok_rows, q_heads, HEAD), cosine, sine_table),
    )
    query_grad = query_grad.reshape(tok_rows, q_heads * HEAD).astype(jnp.bfloat16)
    key_back = normalize_back(key_in, key_inv, k_gain[0], unrotate(kv_total[0], cosine, sine_table))
    key_back = key_back.reshape(tok_rows, kv_width).astype(jnp.bfloat16)
    value_back = kv_total[1].reshape(tok_rows, kv_width).astype(jnp.bfloat16)
    both_back = jnp.concatenate([key_back, value_back], 1)
    grad_rows = lax.psum_scatter(
        lax.dot_general(
            tokens_here, both_back, (((0,), (0,)), ((), ())), preferred_element_type=jnp.float32
        ),
        "ctx",
        scatter_dimension=0,
        tiled=True,
    )
    input_grad = lax.dot_general(
        key_back, key_full, (((1,), (1,)), ((), ())), preferred_element_type=jnp.float32
    )
    input_grad = input_grad + lax.dot_general(
        value_back, value_full, (((1,), (1,)), ((), ())), preferred_element_type=jnp.float32
    )
    passed = shifted(input_grad.astype(jnp.bfloat16), "pipe", -1)
    return (
        query_grad[None],
        grad_rows[:, :kv_width][None],
        grad_rows[:, kv_width:][None],
        passed[None],
    )


def solution(mesh):
    return jax.shard_map(
        local,
        mesh=mesh,
        in_specs=(
            P("pipe", "ctx", None),
            P("pipe", "ctx", None),
            P("pipe", "ctx", None),
            P("pipe", None),
            P("pipe", "ctx", None),
            P("pipe", "ctx", None),
            P("pipe", None),
            P("pipe", None),
        ),
        out_specs=(
            P("pipe", "ctx", None),
            P("pipe", "ctx", None),
            P("pipe", "ctx", None),
            P("pipe", "ctx", None),
        ),
        check_vma=False,
    )
```

profile of v0, /device:TPU:0, one launch (start us, length us, event | category | flops | bytes accessed | tf_op | source)
XLA Modules:
  0.0 868.9 jit_solution(1845894031588987251)
XLA Ops:
  20.3 120.0 %all-gather.7.cloned.1.call-done = bf16[1,4096,512]{2,1,0:T(8,128)(2,1)} async-done(((bf16[1,64,512]{2,1,0:T(8,128)(2,1)}), bf16[1,4096,512]{2,1,0:T(8,128)(2,1)}) %all-gather.7.cloned.1.call-update) | async-done | bytes 4194320 | tf_op jit(solution)/shard_map/all_gather | solution.py:81
  140.3 2.9 fusion.76
  144.0 124.1 %all-gather.5.cloned.1.call-done = bf16[1,4096,512]{2,1,0:T(8,128)(2,1)} async-done(((bf16[1,64,512]{2,1,0:T(8,128)(2,1)}), bf16[1,4096,512]{2,1,0:T(8,128)(2,1)}) %all-gather.5.cloned.1.call-update) | async-done | bytes 4194320 | tf_op jit(solution)/shard_map/all_gather | solution.py:80
  268.1 2.9 fusion.73
  271.8 1.8 multiply_reduce_fusion.2
  277.8 1.5 fusion.116
  282.0 1.7 pad_maximum_fusion.2
  283.7 4.4 collective-permute-start.5
  288.1 6.4 collective-permute-start.4
  294.4 4.0 collective-permute-start.3
  298.4 6.3 collective-permute-start.2
  304.7 4.3 collective-permute-start.1
  309.0 1.7 copy.433
  313.4 2.7 collective-permute-start
  322.7 13.7 %collective-permute-done.1 = bf16[2,128,4,128]{3,1,2,0:T(8,128)(2,1)} collective-permute-done((bf16[2,128,4,128]{3,1,2,0:T(8,128)(2,1)}, bf16[2,128,4,128]{3,1,2,0:T(8,128)(2,1)}, u32[]{:S(2)}, u32[]{:S(2)}) %collective-permute-start.1) | collective-permute-done | bytes 262176 | tf_op jit(solution)/shard_map/ppermute | solution.py:15
  337.6 2.2 collective-permute-done
  348.8 1.5 fusion.61
  366.4 2.5 collective-permute-done.6
  368.9 1.5 collective-permute-start.11
  371.0 10.9 %collective-permute-done.7 = bf16[2,128,4,128]{3,1,2,0:T(8,128)(2,1)S(1)} collective-permute-done((bf16[2,128,4,128]{3,1,2,0:T(8,128)(2,1)S(1)}, bf16[2,128,4,128]{3,1,2,0:T(8,128)(2,1)S(1)}, u32[]{:S(2)}, u32[]{:S(2)}) %collective-permute-start.7) | collective-permute-done | bytes 262176 | tf_op jit(solution)/shard_map/ppermute | solution.py:15
  382.0 9.7 %collective-permute-done.8 = bf16[2,128,4,128]{3,1,2,0:T(8,128)(2,1)S(1)} collective-permute-done((bf16[2,128,4,128]{3,1,2,0:T(8,128)(2,1)S(1)}, bf16[2,128,4,128]{3,1,2,0:T(8,128)(2,1)S(1)}, u32[]{:S(2)}, u32[]{:S(2)}) %collective-permute-start.8) | collective-permute-done | bytes 262176 | tf_op jit(solution)/shard_map/ppermute | solution.py:15
  391.7 9.5 %collective-permute-done.11 = bf16[2,128,4,128]{3,1,2,0:T(8,128)(2,1)S(1)} collective-permute-done((bf16[2,128,4,128]{3,1,2,0:T(8,128)(2,1)S(1)}, bf16[2,128,4,128]{3,1,2,0:T(8,128)(2,1)S(1)}, u32[]{:S(2)}, u32[]{:S(2)}) %collective-permute-start.11) | collective-permute-done | bytes 262176 | tf_op jit(solution)/shard_map/ppermute | solution.py:15
  405.3 9.1 %convolution_bitcast_fusion = f32[4096,1024]{0,1:T(8,128)} fusion(bf16[1,128,4096]{2,1,0:T(8,128)(2,1)S(1)} %copy-done, bf16[128,512]{1,0:T(8,128)(2,1)} %bitcast.613, bf16[128,512]{1,0:T(8,128)(2,1)S(1)} %fusion.115), kind=kOutput, calls=%fused_computation | convolution fusion | flops 1074266112 | bytes 18087936 | tf_op jit(solution)/shard_map/dot_general | solution.py:197
  414.4 17.5 %copy.546 = f32[4096,1024]{1,0:T(8,128)} copy(f32[4096,1024]{0,1:T(8,128)} %convolution_bitcast_fusion) | data formatting | bytes 33554432
  435.5 2.4 mul.515
  448.5 1.9 multiply_add_fusion
  453.5 2.5 fusion
  459.7 2.4 concatenate.48
  462.2 3.1 fusion.105
  465.3 10.3 %collective-permute-done.12 = bf16[128,4096]{1,0:T(8,128)(2,1)} collective-permute-done((bf16[128,4096]{1,0:T(8,128)(2,1)}, bf16[128,4096]{1,0:T(8,128)(2,1)}, u32[]{:S(2)}, u32[]{:S(2)}) %collective-permute-start.12) | collective-permute-done | bytes 1048608 | tf_op jit(solution)/shard_map/ppermute | solution.py:20
  475.6 381.7 %reduce-scatter.4.cloned.1.call-done = f32[64,1024]{1,0:T(8,128)} async-done(((f32[4096,1024]{1,0:T(8,128)}), f32[64,1024]{1,0:T(8,128)}) %reduce-scatter.4.cloned.1.call-update) | async-done | bytes 262160
  860.1 2.3 copy.572
  (223 shorter events, 84.6 us)
Async XLA Ops:
  7.2 133.2 %copy-start = (bf16[1,128,4096]{2,1,0:T(8,128)(2,1)S(1)}, bf16[1,128,4096]{2,1,0:T(8,128)(2,1)}, u32[]{:S(2)}) copy-start(bf16[1,128,4096]{2,1,0:T(8,128)(2,1)} %param.8) | copy-start | bytes 3145732
  7.2 133.1 %all-gather.7.cloned.1.call-start = ((), (), s32[]{:S(2)}) async-start(), calls=%async_computation.2 | async-start | bytes 4259840 | tf_op jit(solution)/shard_map/all_gather | solution.py:81
  7.9 260.2 %all-gather.5.cloned.1.call-start = ((), (), s32[]{:S(2)}) async-start(), calls=%async_computation.1 | async-start | bytes 4259840 | tf_op jit(solution)/shard_map/all_gather | solution.py:80
  8.7 848.6 %reduce-scatter.4.cloned.1.call-start = ((), (), s32[]{:S(2)}) async-start(), calls=%async_computation.3 | async-start | bytes 17039360
  283.7 29.8 %collective-permute-start.5 = (bf16[2,128,4,128]{3,1,2,0:T(8,128)(2,1)}, bf16[2,128,4,128]{3,1,2,0:T(8,128)(2,1)}, u32[]{:S(2)}, u32[]{:S(2)}) collective-permute-start(bf16[2,128,4,128]{3,1,2,0:T(8,128)(2,1)} %pad_maximum_fusion.2), channel_id=1, source_target_pairs={{0,24},{4,28},{8,32},{12,36},{16,40},{20,44},{24,48},{28,52},{32,5... | collective-permute-start | bytes 786440 | tf_op jit(solution)/shard_map/ppermute | solution.py:15
  288.1 29.4 %collective-permute-start.4 = (bf16[2,128,4,128]{3,1,2,0:T(8,128)(2,1)}, bf16[2,128,4,128]{3,1,2,0:T(8,128)(2,1)}, u32[]{:S(2)}, u32[]{:S(2)}) collective-permute-start(bf16[2,128,4,128]{3,1,2,0:T(8,128)(2,1)} %pad_maximum_fusion.2), channel_id=1, source_target_pairs={{0,20},{4,24},{8,28},{12,32},{16,36},{20,40},{24,44},{28,48},{32,5... | collective-permute-start | bytes 786440 | tf_op jit(solution)/shard_map/ppermute | solution.py:15
  294.4 24.3 %collective-permute-start.3 = (bf16[2,128,4,128]{3,1,2,0:T(8,128)(2,1)}, bf16[2,128,4,128]{3,1,2,0:T(8,128)(2,1)}, u32[]{:S(2)}, u32[]{:S(2)}) collective-permute-start(bf16[2,128,4,128]{3,1,2,0:T(8,128)(2,1)} %pad_maximum_fusion.2), channel_id=1, source_target_pairs={{0,16},{4,20},{8,24},{12,28},{16,32},{20,36},{24,40},{28,44},{32,4... | collective-permute-start | bytes 786440 | tf_op jit(solution)/shard_map/ppermute | solution.py:15
  298.4 22.9 %collective-permute-start.2 = (bf16[2,128,4,128]{3,1,2,0:T(8,128)(2,1)}, bf16[2,128,4,128]{3,1,2,0:T(8,128)(2,1)}, u32[]{:S(2)}, u32[]{:S(2)}) collective-permute-start(bf16[2,128,4,128]{3,1,2,0:T(8,128)(2,1)} %pad_maximum_fusion.2), channel_id=1, source_target_pairs={{0,12},{4,16},{8,20},{12,24},{16,28},{20,32},{24,36},{28,40},{32,4... | collective-permute-start | bytes 786440 | tf_op jit(solution)/shard_map/ppermute | solution.py:15
  304.7 31.7 %collective-permute-start.1 = (bf16[2,128,4,128]{3,1,2,0:T(8,128)(2,1)}, bf16[2,128,4,128]{3,1,2,0:T(8,128)(2,1)}, u32[]{:S(2)}, u32[]{:S(2)}) collective-permute-start(bf16[2,128,4,128]{3,1,2,0:T(8,128)(2,1)} %pad_maximum_fusion.2), channel_id=1, source_target_pairs={{0,8},{4,12},{8,16},{12,20},{16,24},{20,28},{24,32},{28,36},{32,40... | collective-permute-start | bytes 786440 | tf_op jit(solution)/shard_map/ppermute | solution.py:15
  312.1 9.3 %copy-start.39 = (pred[128,128]{0,1:T(8,128)(4,1)S(1)}, pred[128,128]{0,1:T(8,128)(4,1)}, u32[]{:S(2)}) copy-start(pred[128,128]{0,1:T(8,128)(4,1)} %get-tuple-element.61) | copy-start | bytes 49156
  312.1 24.3 %copy-start.38 = (pred[128,128]{0,1:T(8,128)(4,1)S(1)}, pred[128,128]{0,1:T(8,128)(4,1)}, u32[]{:S(2)}) copy-start(pred[128,128]{0,1:T(8,128)(4,1)} %get-tuple-element.60) | copy-start | bytes 49156
  313.4 26.4 %copy-start.37 = (pred[128,128]{0,1:T(8,128)(4,1)S(1)}, pred[128,128]{0,1:T(8,128)(4,1)}, u32[]{:S(2)}) copy-start(pred[128,128]{0,1:T(8,128)(4,1)} %get-tuple-element.59) | copy-start | bytes 49156
  313.4 26.4 %collective-permute-start = (bf16[2,128,4,128]{3,1,2,0:T(8,128)(2,1)}, bf16[2,128,4,128]{3,1,2,0:T(8,128)(2,1)S(1)}, u32[]{:S(2)}, u32[]{:S(2)}) collective-permute-start(bf16[2,128,4,128]{3,1,2,0:T(8,128)(2,1)} %pad_maximum_fusion.2), channel_id=1, source_target_pairs={{0,4},{4,8},{8,12},{12,16},{16,20},{20,24},{24,28},{28,32},{32,36}... | collective-permute-start | bytes 786440 | tf_op jit(solution)/shard_map/ppermute | solution.py:15
  339.8 18.8 %copy-start.32 = (bf16[2,128,4,128]{3,1,2,0:T(8,128)(2,1)}, bf16[2,128,4,128]{3,1,2,0:T(8,128)(2,1)S(1)}, u32[]{:S(2)}) copy-start(bf16[2,128,4,128]{3,1,2,0:T(8,128)(2,1)S(1)} %collective-permute-done) | copy-start | bytes 786436
  359.0 7.0 copy-start.13
  359.3 9.6 %collective-permute-start.6 = (bf16[2,128,4,128]{3,1,2,0:T(8,128)(2,1)S(1)}, bf16[2,128,4,128]{3,1,2,0:T(8,128)(2,1)S(1)}, u32[]{:S(2)}, u32[]{:S(2)}) collective-permute-start(bf16[2,128,4,128]{3,1,2,0:T(8,128)(2,1)S(1)} %pad_maximum_fusion.3), channel_id=1, source_target_pairs={{4,0},{8,4},{12,8},{16,12},{20,16},{24,20},{28,24},{32,28},{36,32}... | collective-permute-start | bytes 786440 | tf_op jit(solution)/shard_map/ppermute | solution.py:15
  360.6 21.3 %collective-permute-start.7 = (bf16[2,128,4,128]{3,1,2,0:T(8,128)(2,1)S(1)}, bf16[2,128,4,128]{3,1,2,0:T(8,128)(2,1)S(1)}, u32[]{:S(2)}, u32[]{:S(2)}) collective-permute-start(bf16[2,128,4,128]{3,1,2,0:T(8,128)(2,1)S(1)} %pad_maximum_fusion.4), channel_id=1, source_target_pairs={{8,0},{12,4},{16,8},{20,12},{24,16},{28,20},{32,24},{36,28},{40,32... | collective-permute-start | bytes 786440 | tf_op jit(solution)/shard_map/ppermute | solution.py:15
  362.0 29.7 %collective-permute-start.8 = (bf16[2,128,4,128]{3,1,2,0:T(8,128)(2,1)S(1)}, bf16[2,128,4,128]{3,1,2,0:T(8,128)(2,1)S(1)}, u32[]{:S(2)}, u32[]{:S(2)}) collective-permute-start(bf16[2,128,4,128]{3,1,2,0:T(8,128)(2,1)S(1)} %pad_maximum_fusion.5), channel_id=1, source_target_pairs={{12,0},{16,4},{20,8},{24,12},{28,16},{32,20},{36,24},{40,28},{44,3... | collective-permute-start | bytes 786440 | tf_op jit(solution)/shard_map/ppermute | solution.py:15
  363.3 28.4 %collective-permute-start.9 = (bf16[2,128,4,128]{3,1,2,0:T(8,128)(2,1)S(1)}, bf16[2,128,4,128]{3,1,2,0:T(8,128)(2,1)S(1)}, u32[]{:S(2)}, u32[]{:S(2)}) collective-permute-start(bf16[2,128,4,128]{3,1,2,0:T(8,128)(2,1)S(1)} %pad_maximum_fusion.6), channel_id=1, source_target_pairs={{16,0},{20,4},{24,8},{28,12},{32,16},{36,20},{40,24},{44,28},{48,3... | collective-permute-start | bytes 786440 | tf_op jit(solution)/shard_map/ppermute | solution.py:15
  364.7 27.1 %collective-permute-start.10 = (bf16[2,128,4,128]{3,1,2,0:T(8,128)(2,1)S(1)}, bf16[2,128,4,128]{3,1,2,0:T(8,128)(2,1)S(1)}, u32[]{:S(2)}, u32[]{:S(2)}) collective-permute-start(bf16[2,128,4,128]{3,1,2,0:T(8,128)(2,1)S(1)} %pad_maximum_fusion.7), channel_id=1, source_target_pairs={{20,0},{24,4},{28,8},{32,12},{36,16},{40,20},{44,24},{48,28},{52,3... | collective-permute-start | bytes 786440 | tf_op jit(solution)/shard_map/ppermute | solution.py:15
  366.0 36.4 %copy-start.22 = (f32[128,64]{1,0:T(8,128)S(1)}, f32[128,64]{1,0:T(8,128)}, u32[]{:S(2)}) copy-start(f32[128,64]{1,0:T(8,128)} %copy-done.21) | copy-start | bytes 98308
  366.0 36.4 %copy-start.25 = (f32[128,64]{1,0:T(8,128)S(1)}, f32[128,64]{1,0:T(8,128)}, u32[]{:S(2)}) copy-start(f32[128,64]{1,0:T(8,128)} %copy-done.24) | copy-start | bytes 98308
  366.4 36.1 %copy-start.43 = (f32[1,128]{1,0:T(1,128)S(1)}, f32[1,128]{1,0:T(1,128)}, u32[]{:S(2)}) copy-start(f32[1,128]{1,0:T(1,128)} %param.15) | copy-start | bytes 1540
  368.9 32.3 %collective-permute-start.11 = (bf16[2,128,4,128]{3,1,2,0:T(8,128)(2,1)S(1)}, bf16[2,128,4,128]{3,1,2,0:T(8,128)(2,1)S(1)}, u32[]{:S(2)}, u32[]{:S(2)}) collective-permute-start(bf16[2,128,4,128]{3,1,2,0:T(8,128)(2,1)S(1)} %pad_maximum_fusion.8), channel_id=1, source_target_pairs={{24,0},{28,4},{32,8},{36,12},{40,16},{44,20},{48,24},{52,28},{56,3... | collective-permute-start | bytes 786440 | tf_op jit(solution)/shard_map/ppermute | solution.py:15
  370.7 34.5 %copy-start.41 = (f32[512]{0:T(512)S(1)}, f32[512]{0:T(512)}, u32[]{:S(2)}) copy-start(f32[512]{0:T(512)} %broadcast_bitcast_fusion.1) | copy-start | bytes 6148
  401.7 12.8 %copy-start.27 = (bf16[1,128,4,128]{3,2,1,0:T(4,128)(2,1)}, bf16[1,128,4,128]{3,2,1,0:T(4,128)(2,1)S(1)}, u32[]{:S(2)}) copy-start(bf16[1,128,4,128]{3,2,1,0:T(4,128)(2,1)S(1)} %copy.421) | copy-start | bytes 393220
  405.3 9.1 %copy-start.29 = (bf16[128,512]{1,0:T(8,128)(2,1)}, bf16[128,512]{1,0:T(8,128)(2,1)S(1)}, u32[]{:S(2)}) copy-start(bf16[128,512]{1,0:T(8,128)(2,1)S(1)} %fusion.115) | copy-start | bytes 393220
  433.1 6.8 copy-start.11
  434.2 7.0 copy-start.9
  435.5 6.9 copy-start.7
  455.9 19.6 %collective-permute-start.12 = (bf16[128,4096]{1,0:T(8,128)(2,1)}, bf16[128,4096]{1,0:T(8,128)(2,1)}, u32[]{:S(2)}, u32[]{:S(2)}) collective-permute-start(bf16[128,4096]{1,0:T(8,128)(2,1)} %fusion), channel_id=1, source_target_pairs={{0,3},{1,0},{2,1},{3,2},{4,7},{5,4},{6,5},{7,6},{8,11},{9,8},{10,9... | collective-permute-start | bytes 3145736 | tf_op jit(solution)/shard_map/ppermute | solution.py:20
  459.7 402.6 %copy-start.1 = (bf16[1,128,4096]{2,1,0:T(8,128)(2,1)S(1)}, bf16[1,128,4096]{2,1,0:T(8,128)(2,1)}, u32[]{:S(2)}) copy-start(bf16[1,128,4096]{2,1,0:T(8,128)(2,1)} %param.8) | copy-start | bytes 3145732
  (30 other events, 115.4 us)
Sparse Core Ops, SparseCore 0:
  11.6 128.6 all-gather.6
  143.9 124.1 all-gather.4
  432.0 425.1 reduce-scatter.3
where the time goes:
time: 871 us; the launch traced here: 869 us
  waiting for transfers between devices  687 us (79%)
  local copies, waits for them, and re-layouts  55.3 us (6%)
  matrix products  52.3 us (6%)
  starting transfers between devices  37.1 us (4%)
  other arithmetic  22 us (3%)
  between operations  14.8 us (2%)
    unnamed x4, waiting for transfers between devices  383 us
    all_gather x1, waiting for transfers between devices, local(): lax.all_gather(w_key[0], 'ctx', axis=0, tiled=True)  124 us
    all_gather x1, waiting for transfers between devices, local(): lax.all_gather(w_value[0], 'ctx', axis=0, tiled=True)  120 us
    ppermute x12, waiting for transfers between devices, passed_along(): return lax.ppermute(block, axis, route)  50 us
    ppermute x12, starting transfers between devices, passed_along(): return lax.ppermute(block, axis, route)  36 us
    unnamed x104, local copies, waits for them, and re-layouts  32.2 us
  transfers between devices with their start and end apart: 16, of which 11 were waited for; matrix products, arithmetic and copies ran while one was open for 6% of the time, Pallas kernels for 0%

commit v1 on v0

--- a/solution.py
+++ b/solution.py
@@ -77,7 +77,9 @@
     reach_blocks = WINDOW // tok_rows
     ctx_index = lax.axis_index("ctx")
     key_full, value_full = (
-        lax.all_gather(w_key[0], "ctx", axis=0, tiled=True),
+        jnp.concatenate(
+            lax.all_to_all(jnp.stack([w_key[0]] * lax.axis_size("ctx")), "ctx", 0, 0), axis=0
+        ),
         lax.all_gather(w_value[0], "ctx", axis=0, tiled=True),
     )
     key_raw = jnp.dot(tokens_here, key_full, preferred_element_type=jnp.float32).astype(

time: 871 us -> 776 us (0.89)
  waiting for transfers between devices: 687 us -> 574 us
  starting transfers between devices: 37.1 us -> 52.1 us
    all_gather x1 -> x0, waiting for transfers between devices: 124 us -> none  [local(): lax.all_gather(w_key[0], 'ctx', axis=0, tiled=True)]
    all_to_all x0 -> x1, starting transfers between devices: none -> 13.3 us  [local(): lax.all_to_all(jnp.stack([w_key[0]] * lax.axis_size('ctx')), 'ctx', 0, 0)]
    unnamed x4 -> x3, waiting for transfers between devices: 383 us -> 384 us
  transfers between devices with their start and end apart: 16 -> 16, of which waited for: 11 -> 9; matrix products, arithmetic and copies ran while one was open for 6% -> 8% of each run, Pallas kernels for 0% -> 0%
where the time goes in v1:
time: 776 us; the launch traced here: 773 us
  waiting for transfers between devices  574 us (74%)
  local copies, waits for them, and re-layouts  55.9 us (7%)
  matrix products  55.3 us (7%)
  starting transfers between devices  52.1 us (7%)
  other arithmetic  20.8 us (3%)
  between operations  15.2 us (2%)
    unnamed x3, waiting for transfers between devices  384 us
    all_gather x1, waiting for transfers between devices, local(): lax.all_gather(w_value[0], 'ctx', axis=0, tiled=True)  123 us
    ppermute x12, waiting for transfers between devices, passed_along(): return lax.ppermute(block, axis, route)  57 us
    ppermute x12, starting transfers between devices, passed_along(): return lax.ppermute(block, axis, route)  38.8 us
    unnamed x104, local copies, waits for them, and re-layouts  29.5 us
  transfers between devices with their start and end apart: 16, of which 9 were waited for; matrix products, arithmetic and copies ran while one was open for 8% of the time, Pallas kernels for 0%

profile of v1, /device:TPU:0, one launch (start us, length us, event | category | flops | bytes accessed | tf_op | source)
XLA Modules:
  0.0 773.4 jit_solution(7276952949627030441)
XLA Ops:
  7.9 3.3 stack.88
  11.2 13.3 %all-to-all-start = ((bf16[64,64,512]{2,1,0:T(8,128)(2,1)}), bf16[64,64,512]{2,1,0:T(8,128)(2,1)}, u32[]{:S(2)}, u32[]{:S(2)}) async-start(bf16[64,64,512]{2,1,0:T(8,128)(2,1)} %stack.88), calls=%async_computation | async-start | bytes 8388608 | tf_op jit(solution)/shard_map/all_to_all | solution.py:81
  34.0 123.2 %all-gather.3.cloned.1.call-done = bf16[1,4096,512]{2,1,0:T(8,128)(2,1)} async-done(((bf16[1,64,512]{2,1,0:T(8,128)(2,1)}), bf16[1,4096,512]{2,1,0:T(8,128)(2,1)}) %all-gather.3.cloned.1.call-update) | async-done | bytes 4194320 | tf_op jit(solution)/shard_map/all_gather | solution.py:83
  157.2 2.9 fusion.66
  161.0 2.9 fusion.69
  164.7 1.8 multiply_reduce_fusion.2
  170.6 1.5 fusion.107
  174.8 1.7 pad_maximum_fusion.2
  176.5 4.1 collective-permute-start.5
  180.7 5.8 collective-permute-start.4
  186.4 3.8 collective-permute-start.3
  190.3 6.7 collective-permute-start.2
  197.0 5.0 collective-permute-start
  201.9 1.7 copy.433
  206.4 14.2 %collective-permute-done = bf16[2,128,4,128]{3,1,2,0:T(8,128)(2,1)} collective-permute-done((bf16[2,128,4,128]{3,1,2,0:T(8,128)(2,1)}, bf16[2,128,4,128]{3,1,2,0:T(8,128)(2,1)}, u32[]{:S(2)}, u32[]{:S(2)}) %collective-permute-start) | collective-permute-done | bytes 262176 | tf_op jit(solution)/shard_map/ppermute | solution.py:15
  220.6 5.4 collective-permute-start.1
  227.3 6.0 collective-permute-done.1
  265.8 4.9 collective-permute-done.6
  272.9 9.9 %collective-permute-done.7 = bf16[2,128,4,128]{3,1,2,0:T(8,128)(2,1)S(1)} collective-permute-done((bf16[2,128,4,128]{3,1,2,0:T(8,128)(2,1)S(1)}, bf16[2,128,4,128]{3,1,2,0:T(8,128)(2,1)S(1)}, u32[]{:S(2)}, u32[]{:S(2)}) %collective-permute-start.7) | collective-permute-done | bytes 262176 | tf_op jit(solution)/shard_map/ppermute | solution.py:15
  282.8 10.0 %collective-permute-done.8 = bf16[2,128,4,128]{3,1,2,0:T(8,128)(2,1)S(1)} collective-permute-done((bf16[2,128,4,128]{3,1,2,0:T(8,128)(2,1)S(1)}, bf16[2,128,4,128]{3,1,2,0:T(8,128)(2,1)S(1)}, u32[]{:S(2)}, u32[]{:S(2)}) %collective-permute-start.8) | collective-permute-done | bytes 262176 | tf_op jit(solution)/shard_map/ppermute | solution.py:15
  292.8 11.9 %collective-permute-done.11 = bf16[2,128,4,128]{3,1,2,0:T(8,128)(2,1)S(1)} collective-permute-done((bf16[2,128,4,128]{3,1,2,0:T(8,128)(2,1)S(1)}, bf16[2,128,4,128]{3,1,2,0:T(8,128)(2,1)S(1)}, u32[]{:S(2)}, u32[]{:S(2)}) %collective-permute-start.11) | collective-permute-done | bytes 262176 | tf_op jit(solution)/shard_map/ppermute | solution.py:15
  308.7 9.1 %convolution_bitcast_fusion = f32[4096,1024]{0,1:T(8,128)} fusion(bf16[1,128,4096]{2,1,0:T(8,128)(2,1)S(1)} %copy-done, bf16[128,512]{1,0:T(8,128)(2,1)} %bitcast.608, bf16[128,512]{1,0:T(8,128)(2,1)S(1)} %fusion.106), kind=kOutput, calls=%fused_computation | convolution fusion | flops 1074266112 | bytes 18087936 | tf_op jit(solution)/shard_map/dot_general | solution.py:199
  317.9 17.5 %copy.546 = f32[4096,1024]{1,0:T(8,128)} copy(f32[4096,1024]{0,1:T(8,128)} %convolution_bitcast_fusion) | data formatting | bytes 33554432
  339.0 2.4 mul.515
  351.9 1.8 multiply_add_fusion
  353.7 3.8 fusion.165
  357.5 2.5 fusion
  362.8 2.5 concatenate.48
  365.2 3.1 fusion.96
  368.3 9.9 %collective-permute-done.12 = bf16[128,4096]{1,0:T(8,128)(2,1)} collective-permute-done((bf16[128,4096]{1,0:T(8,128)(2,1)}, bf16[128,4096]{1,0:T(8,128)(2,1)}, u32[]{:S(2)}, u32[]{:S(2)}) %collective-permute-start.12) | collective-permute-done | bytes 1048608 | tf_op jit(solution)/shard_map/ppermute | solution.py:20
  378.3 383.2 %reduce-scatter.4.cloned.1.call-done = f32[64,1024]{1,0:T(8,128)} async-done(((f32[4096,1024]{1,0:T(8,128)}), f32[64,1024]{1,0:T(8,128)}) %reduce-scatter.4.cloned.1.call-update) | async-done | bytes 262160
  764.2 2.3 copy.572
  (223 shorter events, 80.1 us)
Async XLA Ops:
  7.2 150.1 %copy-start = (bf16[1,128,4096]{2,1,0:T(8,128)(2,1)S(1)}, bf16[1,128,4096]{2,1,0:T(8,128)(2,1)}, u32[]{:S(2)}) copy-start(bf16[1,128,4096]{2,1,0:T(8,128)(2,1)} %param.8) | copy-start | bytes 3145732
  7.2 150.0 %all-gather.3.cloned.1.call-start = ((), (), s32[]{:S(2)}) async-start(), calls=%async_computation.2 | async-start | bytes 4259840 | tf_op jit(solution)/shard_map/all_gather | solution.py:83
  11.2 13.4 %copy-start.36 = (bf16[1,128,2048]{2,1,0:T(8,128)(2,1)S(1)}, bf16[1,128,2048]{2,1,0:T(8,128)(2,1)}, u32[]{:S(2)}) copy-start(bf16[1,128,2048]{2,1,0:T(8,128)(2,1)} %param.10) | copy-start | bytes 1572868
  11.2 13.6 %copy-start.19 = (bf16[1,128,2048]{2,1,0:T(8,128)(2,1)S(1)}, bf16[1,128,2048]{2,1,0:T(8,128)(2,1)}, u32[]{:S(2)}) copy-start(bf16[1,128,2048]{2,1,0:T(8,128)(2,1)} %param.9) | copy-start | bytes 1572868
  11.2 149.7 %all-to-all-start = ((bf16[64,64,512]{2,1,0:T(8,128)(2,1)}), bf16[64,64,512]{2,1,0:T(8,128)(2,1)}, u32[]{:S(2)}, u32[]{:S(2)}) async-start(bf16[64,64,512]{2,1,0:T(8,128)(2,1)} %stack.88), calls=%async_computation | async-start | bytes 8388608 | tf_op jit(solution)/shard_map/all_to_all | solution.py:81
  24.5 736.9 %reduce-scatter.4.cloned.1.call-start = ((), (), s32[]{:S(2)}) async-start(), calls=%async_computation.3 | async-start | bytes 17039360
  176.5 61.8 %collective-permute-start.5 = (bf16[2,128,4,128]{3,1,2,0:T(8,128)(2,1)}, bf16[2,128,4,128]{3,1,2,0:T(8,128)(2,1)}, u32[]{:S(2)}, u32[]{:S(2)}) collective-permute-start(bf16[2,128,4,128]{3,1,2,0:T(8,128)(2,1)} %pad_maximum_fusion.2), channel_id=1, source_target_pairs={{0,24},{4,28},{8,32},{12,36},{16,40},{20,44},{24,48},{28,52},{32,5... | collective-permute-start | bytes 786440 | tf_op jit(solution)/shard_map/ppermute | solution.py:15
  180.7 56.4 %collective-permute-start.4 = (bf16[2,128,4,128]{3,1,2,0:T(8,128)(2,1)}, bf16[2,128,4,128]{3,1,2,0:T(8,128)(2,1)}, u32[]{:S(2)}, u32[]{:S(2)}) collective-permute-start(bf16[2,128,4,128]{3,1,2,0:T(8,128)(2,1)} %pad_maximum_fusion.2), channel_id=1, source_target_pairs={{0,20},{4,24},{8,28},{12,32},{16,36},{20,40},{24,44},{28,48},{32,5... | collective-permute-start | bytes 786440 | tf_op jit(solution)/shard_map/ppermute | solution.py:15
  186.4 49.3 %collective-permute-start.3 = (bf16[2,128,4,128]{3,1,2,0:T(8,128)(2,1)}, bf16[2,128,4,128]{3,1,2,0:T(8,128)(2,1)}, u32[]{:S(2)}, u32[]{:S(2)}) collective-permute-start(bf16[2,128,4,128]{3,1,2,0:T(8,128)(2,1)} %pad_maximum_fusion.2), channel_id=1, source_target_pairs={{0,16},{4,20},{8,24},{12,28},{16,32},{20,36},{24,40},{28,44},{32,4... | collective-permute-start | bytes 786440 | tf_op jit(solution)/shard_map/ppermute | solution.py:15
  190.3 44.2 %collective-permute-start.2 = (bf16[2,128,4,128]{3,1,2,0:T(8,128)(2,1)}, bf16[2,128,4,128]{3,1,2,0:T(8,128)(2,1)}, u32[]{:S(2)}, u32[]{:S(2)}) collective-permute-start(bf16[2,128,4,128]{3,1,2,0:T(8,128)(2,1)} %pad_maximum_fusion.2), channel_id=1, source_target_pairs={{0,12},{4,16},{8,20},{12,24},{16,28},{20,32},{24,36},{28,40},{32,4... | collective-permute-start | bytes 786440 | tf_op jit(solution)/shard_map/ppermute | solution.py:15
  197.0 23.6 %collective-permute-start = (bf16[2,128,4,128]{3,1,2,0:T(8,128)(2,1)}, bf16[2,128,4,128]{3,1,2,0:T(8,128)(2,1)}, u32[]{:S(2)}, u32[]{:S(2)}) collective-permute-start(bf16[2,128,4,128]{3,1,2,0:T(8,128)(2,1)} %pad_maximum_fusion.2), channel_id=1, source_target_pairs={{0,4},{4,8},{8,12},{12,16},{16,20},{20,24},{24,28},{28,32},{32,36}... | collective-permute-start | bytes 786440 | tf_op jit(solution)/shard_map/ppermute | solution.py:15
  205.0 29.4 %copy-start.40 = (pred[128,128]{0,1:T(8,128)(4,1)S(1)}, pred[128,128]{0,1:T(8,128)(4,1)}, u32[]{:S(2)}) copy-start(pred[128,128]{0,1:T(8,128)(4,1)} %get-tuple-element.61) | copy-start | bytes 49156
  205.0 30.7 %copy-start.39 = (pred[128,128]{0,1:T(8,128)(4,1)S(1)}, pred[128,128]{0,1:T(8,128)(4,1)}, u32[]{:S(2)}) copy-start(pred[128,128]{0,1:T(8,128)(4,1)} %get-tuple-element.62) | copy-start | bytes 49156
  205.0 32.0 %copy-start.38 = (pred[128,128]{0,1:T(8,128)(4,1)S(1)}, pred[128,128]{0,1:T(8,128)(4,1)}, u32[]{:S(2)}) copy-start(pred[128,128]{0,1:T(8,128)(4,1)} %get-tuple-element.63) | copy-start | bytes 49156
  220.6 12.7 %collective-permute-start.1 = (bf16[2,128,4,128]{3,1,2,0:T(8,128)(2,1)}, bf16[2,128,4,128]{3,1,2,0:T(8,128)(2,1)S(1)}, u32[]{:S(2)}, u32[]{:S(2)}) collective-permute-start(bf16[2,128,4,128]{3,1,2,0:T(8,128)(2,1)} %pad_maximum_fusion.2), channel_id=1, source_target_pairs={{0,8},{4,12},{8,16},{12,20},{16,24},{20,28},{24,32},{28,36},{32,40... | collective-permute-start | bytes 786440 | tf_op jit(solution)/shard_map/ppermute | solution.py:15
  233.3 22.4 %copy-start.32 = (bf16[2,128,4,128]{3,1,2,0:T(8,128)(2,1)}, bf16[2,128,4,128]{3,1,2,0:T(8,128)(2,1)S(1)}, u32[]{:S(2)}) copy-start(bf16[2,128,4,128]{3,1,2,0:T(8,128)(2,1)S(1)} %collective-permute-done.1) | copy-start | bytes 786436
  258.7 12.0 %collective-permute-start.6 = (bf16[2,128,4,128]{3,1,2,0:T(8,128)(2,1)S(1)}, bf16[2,128,4,128]{3,1,2,0:T(8,128)(2,1)S(1)}, u32[]{:S(2)}, u32[]{:S(2)}) collective-permute-start(bf16[2,128,4,128]{3,1,2,0:T(8,128)(2,1)S(1)} %pad_maximum_fusion.3), channel_id=1, source_target_pairs={{4,0},{8,4},{12,8},{16,12},{20,16},{24,20},{28,24},{32,28},{36,32}... | collective-permute-start | bytes 786440 | tf_op jit(solution)/shard_map/ppermute | solution.py:15
  260.0 22.7 %collective-permute-start.7 = (bf16[2,128,4,128]{3,1,2,0:T(8,128)(2,1)S(1)}, bf16[2,128,4,128]{3,1,2,0:T(8,128)(2,1)S(1)}, u32[]{:S(2)}, u32[]{:S(2)}) collective-permute-start(bf16[2,128,4,128]{3,1,2,0:T(8,128)(2,1)S(1)} %pad_maximum_fusion.4), channel_id=1, source_target_pairs={{8,0},{12,4},{16,8},{20,12},{24,16},{28,20},{32,24},{36,28},{40,32... | collective-permute-start | bytes 786440 | tf_op jit(solution)/shard_map/ppermute | solution.py:15
  261.4 31.4 %collective-permute-start.8 = (bf16[2,128,4,128]{3,1,2,0:T(8,128)(2,1)S(1)}, bf16[2,128,4,128]{3,1,2,0:T(8,128)(2,1)S(1)}, u32[]{:S(2)}, u32[]{:S(2)}) collective-permute-start(bf16[2,128,4,128]{3,1,2,0:T(8,128)(2,1)S(1)} %pad_maximum_fusion.5), channel_id=1, source_target_pairs={{12,0},{16,4},{20,8},{24,12},{28,16},{32,20},{36,24},{40,28},{44,3... | collective-permute-start | bytes 786440 | tf_op jit(solution)/shard_map/ppermute | solution.py:15
  262.7 30.0 %collective-permute-start.9 = (bf16[2,128,4,128]{3,1,2,0:T(8,128)(2,1)S(1)}, bf16[2,128,4,128]{3,1,2,0:T(8,128)(2,1)S(1)}, u32[]{:S(2)}, u32[]{:S(2)}) collective-permute-start(bf16[2,128,4,128]{3,1,2,0:T(8,128)(2,1)S(1)} %pad_maximum_fusion.6), channel_id=1, source_target_pairs={{16,0},{20,4},{24,8},{28,12},{32,16},{36,20},{40,24},{44,28},{48,3... | collective-permute-start | bytes 786440 | tf_op jit(solution)/shard_map/ppermute | solution.py:15
  264.0 28.7 %collective-permute-start.10 = (bf16[2,128,4,128]{3,1,2,0:T(8,128)(2,1)S(1)}, bf16[2,128,4,128]{3,1,2,0:T(8,128)(2,1)S(1)}, u32[]{:S(2)}, u32[]{:S(2)}) collective-permute-start(bf16[2,128,4,128]{3,1,2,0:T(8,128)(2,1)S(1)} %pad_maximum_fusion.7), channel_id=1, source_target_pairs={{20,0},{24,4},{28,8},{32,12},{36,16},{40,20},{44,24},{48,28},{52,3... | collective-permute-start | bytes 786440 | tf_op jit(solution)/shard_map/ppermute | solution.py:15
  265.4 40.4 %copy-start.22 = (f32[128,64]{1,0:T(8,128)S(1)}, f32[128,64]{1,0:T(8,128)}, u32[]{:S(2)}) copy-start(f32[128,64]{1,0:T(8,128)} %copy-done.21) | copy-start | bytes 98308
  265.4 40.4 %copy-start.25 = (f32[128,64]{1,0:T(8,128)S(1)}, f32[128,64]{1,0:T(8,128)}, u32[]{:S(2)}) copy-start(f32[128,64]{1,0:T(8,128)} %copy-done.24) | copy-start | bytes 98308
  265.8 7.1 copy-start.3
  265.8 40.1 %copy-start.43 = (f32[1,128]{1,0:T(1,128)S(1)}, f32[1,128]{1,0:T(1,128)}, u32[]{:S(2)}) copy-start(f32[1,128]{1,0:T(1,128)} %param.15) | copy-start | bytes 1540
  270.7 33.9 %collective-permute-start.11 = (bf16[2,128,4,128]{3,1,2,0:T(8,128)(2,1)S(1)}, bf16[2,128,4,128]{3,1,2,0:T(8,128)(2,1)S(1)}, u32[]{:S(2)}, u32[]{:S(2)}) collective-permute-start(bf16[2,128,4,128]{3,1,2,0:T(8,128)(2,1)S(1)} %pad_maximum_fusion.8), channel_id=1, source_target_pairs={{24,0},{28,4},{32,8},{36,12},{40,16},{44,20},{48,24},{52,28},{56,3... | collective-permute-start | bytes 786440 | tf_op jit(solution)/shard_map/ppermute | solution.py:15
  272.5 36.0 %copy-start.41 = (f32[512]{0:T(512)S(1)}, f32[512]{0:T(512)}, u32[]{:S(2)}) copy-start(f32[512]{0:T(512)} %broadcast_bitcast_fusion.1) | copy-start | bytes 6148
  305.1 12.8 %copy-start.27 = (bf16[1,128,4,128]{3,2,1,0:T(4,128)(2,1)}, bf16[1,128,4,128]{3,2,1,0:T(4,128)(2,1)S(1)}, u32[]{:S(2)}) copy-start(bf16[1,128,4,128]{3,2,1,0:T(4,128)(2,1)S(1)} %copy.421) | copy-start | bytes 393220
  308.7 9.1 %copy-start.29 = (bf16[128,512]{1,0:T(8,128)(2,1)}, bf16[128,512]{1,0:T(8,128)(2,1)S(1)}, u32[]{:S(2)}) copy-start(bf16[128,512]{1,0:T(8,128)(2,1)S(1)} %fusion.106) | copy-start | bytes 393220
  337.7 7.0 copy-start.8
  360.0 18.3 %collective-permute-start.12 = (bf16[128,4096]{1,0:T(8,128)(2,1)}, bf16[128,4096]{1,0:T(8,128)(2,1)}, u32[]{:S(2)}, u32[]{:S(2)}) collective-permute-start(bf16[128,4096]{1,0:T(8,128)(2,1)} %fusion), channel_id=1, source_target_pairs={{0,3},{1,0},{2,1},{3,2},{4,7},{5,4},{6,5},{7,6},{8,11},{9,8},{10,9... | collective-permute-start | bytes 3145736 | tf_op jit(solution)/shard_map/ppermute | solution.py:20
  362.8 403.7 %copy-start.1 = (bf16[1,128,4096]{2,1,0:T(8,128)(2,1)S(1)}, bf16[1,128,4096]{2,1,0:T(8,128)(2,1)}, u32[]{:S(2)}) copy-start(bf16[1,128,4096]{2,1,0:T(8,128)(2,1)} %param.8) | copy-start | bytes 3145732
  (30 other events, 120.8 us)
Sparse Core Ops, SparseCore 0:
  11.6 145.5 all-gather.2
  335.5 425.9 reduce-scatter.3
